TPU v7x, 256 devices: a whole 4x4x8 slice. The times are simulated.
256 devices in a mesh: sub: 16 (over z, core), fr: 16 (over y, x).
Axes of the slice: x: 4, y: 4, z: 8, core: 2. Of those that a mesh axis runs over, the one named last changes fastest.
Arguments:
- front_leaf: bfloat16 [32768, 2048], P(('sub', 'fr')), as said below
- shares_one: float32 [32768, 384], P(('sub', 'fr')), as said below
- shares_two: float32 [32768, 384], P(('sub', 'fr')), as said below
- map_leaf: int32 [16, 13], P('sub'), may hold values from 0 to 15, as said below
- map_mid: int32 [8, 13], replicated, may hold values from 0 to 15, as said below
Outputs:
- leaf_panel: float32 [32768, 384], P(('sub', 'fr'))
- middle_panel: float32 [32768, 384], P(('sub', 'fr'))
- top_panel: float32 [32768, 384], P(('sub', 'fr'))
- contribution: float32 [32768, 1664], P(('sub', 'fr'))
Inputs may be any that keep to these rules, and one draw needn't show every extreme that they name: `front_leaf`: each block of 2048 rows is a symmetric positive definite front. `shares_one`: in each block of 2048 rows the first 384 rows are symmetric; with the extended contributions every middle front is positive definite. `shares_two`: in each block of 2048 rows the first 384 rows are symmetric; with the extended contributions every top front is positive definite. `map_leaf`: each row lists 13 different blocks; rows 2q and 2q+1 together name every block of their parent. `map_mid`: each row lists 13 different blocks; rows 2r and 2r+1 together name every block of their parent.
All inputs are finite; a program needn't handle non-finite values.
Results may differ from a plain program's by a relative error of at most 0.0003.
Values sent between devices are 32-bit elements; how exact they have to be, the bound alone decides.
No kernel may reach another device: no remote copies, remote signals or barrier semaphores. Data moves between devices by JAX's collectives and lax.ppermute only.
A program may use at most 128 MiB of HBM per device.

v0:
```python
import jax
import jax.numpy as jnp
from jax import lax
from jax.sharding import PartitionSpec as P

BLK = 128
P_SIZE = 384
NFB = 16
NPB = 3
HIGH = lax.Precision.HIGHEST


def partner(array, axis, stride):
    return lax.ppermute(array, axis, [(i, i ^ 1 << stride) for i in range(lax.axis_size(axis))])


def eliminate(front, row_start):
    row_count, front_order = front.shape
    panels = []
    for block_index in range(NPB):
        block_low = block_index * BLK
        gathered = lax.all_gather(front[:, block_low : block_low + BLK], "fr", axis=0, tiled=True)
        row_ids = jnp.arange(front_order)
        lower_block = jnp.linalg.cholesky(gathered[block_low : block_low + BLK])
        solved = lax.linalg.triangular_solve(
            lower_block, gathered, left_side=False, lower=True, transpose_a=True
        )
        below = jnp.where((row_ids >= block_low + BLK)[:, None], solved, 0.0)
        placed = below.at[block_low : block_low + BLK].set(lower_block)
        own_below = lax.dynamic_slice_in_dim(below, row_start, row_count, 0)
        own_panel = lax.dynamic_slice_in_dim(placed, row_start, row_count, 0)
        front = front - jnp.dot(
            own_below, below.T, precision=HIGH, preferred_element_type=jnp.float32
        )
        panels.append(own_panel)
    return (jnp.concatenate(panels, axis=1), front)


def make_table(block_map):
    padded = jnp.concatenate([jnp.full((NPB,), -1, jnp.int32), block_map])
    return (padded[:, None] == jnp.arange(NFB, dtype=jnp.int32)[None, :]).astype(jnp.float32)


def extend(front, block_map, row_start):
    row_count, front_order = front.shape
    block_share = row_count // BLK
    block_table = make_table(block_map)
    padded = jnp.concatenate([jnp.full((NPB,), -1, jnp.int32), block_map])
    parents = row_start // BLK + jnp.arange(block_share)
    matches = padded[None, :] == parents[:, None]
    present = jnp.any(matches, axis=1)
    source_block = jnp.sum(jnp.where(matches, jnp.arange(NFB)[None, :], 0), axis=1)
    source_rows = (source_block[:, None] * BLK + jnp.arange(BLK)[None, :]).reshape(row_count)
    is_live = jnp.repeat(present, BLK)
    shard_rows = lax.all_gather(front, "fr", axis=0, tiled=True)
    inside = is_live & (source_rows >= 0) & (source_rows < shard_rows.shape[0])
    picked_rows = jnp.take(shard_rows, jnp.clip(source_rows, 0, shard_rows.shape[0] - 1), axis=0)
    picked_rows = jnp.where(inside[:, None], picked_rows, 0.0)
    mapped = jnp.einsum(
        "rqc,qe->rec", picked_rows.reshape(row_count, NFB, BLK), block_table, precision=HIGH
    )
    return mapped.reshape(row_count, front_order)


def combine(front, shares, block_map, row_start, level_bit):
    front_order = front.shape[1]
    piece_part = extend(front, block_map, row_start) + jnp.pad(
        shares, ((0, 0), (0, front_order - P_SIZE))
    )
    return piece_part + partner(piece_part, "sub", level_bit)


def local(front_leaf, shares_one, shares_two, map_leaf, map_mid):
    row_count = front_leaf.shape[0]
    row_start = lax.axis_index("fr") * row_count
    sub_index = lax.axis_index("sub")
    leaf_panel, child_front = eliminate(front_leaf.astype(jnp.float32), row_start)
    shares_sum = shares_two + partner(shares_two, "sub", 0)
    middle_front = combine(child_front, shares_one, map_leaf[0], row_start, 0)
    middle_panel, middle_front = eliminate(middle_front, row_start)
    pair_map = lax.dynamic_index_in_dim(map_mid, sub_index // 2, 0, keepdims=False)
    top_front = combine(middle_front, shares_sum, pair_map, row_start, 1)
    top_panel, top_front = eliminate(top_front, row_start)
    row_ids = row_start + jnp.arange(row_count)
    contribution = jnp.where((row_ids >= P_SIZE)[:, None], top_front[:, P_SIZE:], 0.0)
    return (leaf_panel, middle_panel, top_panel, contribution)


def solution(mesh):
    in_specs = (
        P(("sub", "fr"), None),
        P(("sub", "fr"), None),
        P(("sub", "fr"), None),
        P("sub", None),
        P(),
    )
    out_specs = (
        P(("sub", "fr"), None),
        P(("sub", "fr"), None),
        P(("sub", "fr"), None),
        P(("sub", "fr"), None),
    )
    return jax.shard_map(local, mesh=mesh, in_specs=in_specs, out_specs=out_specs, check_vma=False)
```

profile of v0, /device:TPU:2, one launch (start us, length us, event | category | flops | bytes accessed | tf_op | source)
XLA Modules:
  0.0 1077.1 jit_solution(2914424873114445792)
XLA Ops:
  9.3 52.5 %all-gather.12.cloned.1.call-done = f32[2048,128]{0,1:T(8,128)} async-done(((f32[128,128]{0,1:T(8,128)}), f32[2048,128]{0,1:T(8,128)}) %all-gather.12.cloned.1.call-update) | async-done | bytes 1048592 | tf_op jit(solution)/shard_map/all_gather | solution.py:22
  63.6 11.7 %cholesky.149 = f32[128,128]{1,0:T(8,128)S(1)} custom-call(f32[128,128]{1,0:T(8,128)S(1)} %fusion.29), custom_call_target="Cholesky" | custom-call | tf_op jit(solution)/shard_map/jit(cholesky)/cholesky | solution.py:24
  76.6 9.8 custom-call.13
  86.5 2.3 fusion.8
  88.7 1.8 convolution_subtract_fusion.7
  91.5 47.4 %all-gather.14.cloned.1.call-done = f32[2048,128]{0,1:T(8,128)} async-done(((f32[128,128]{0,1:T(8,128)}), f32[2048,128]{0,1:T(8,128)}) %all-gather.14.cloned.1.call-update) | async-done | bytes 1048592 | tf_op jit(solution)/shard_map/all_gather | solution.py:22
  140.7 11.7 %cholesky.160 = f32[128,128]{1,0:T(8,128)S(1)} custom-call(f32[128,128]{1,0:T(8,128)S(1)} %fusion.27), custom_call_target="Cholesky" | custom-call | tf_op jit(solution)/shard_map/jit(cholesky)/cholesky | solution.py:24
  153.8 9.8 custom-call.14
  163.6 2.3 fusion.7
  165.8 1.8 convolution_subtract_fusion.6
  169.8 47.2 %all-gather.16.cloned.1.call-done = f32[2048,128]{0,1:T(8,128)} async-done(((f32[128,128]{0,1:T(8,128)}), f32[2048,128]{0,1:T(8,128)}) %all-gather.16.cloned.1.call-update) | async-done | bytes 1048592 | tf_op jit(solution)/shard_map/all_gather | solution.py:22
  218.8 11.7 %cholesky.171 = f32[128,128]{1,0:T(8,128)S(1)} custom-call(f32[128,128]{1,0:T(8,128)S(1)} %fusion.25), custom_call_target="Cholesky" | custom-call | tf_op jit(solution)/shard_map/jit(cholesky)/cholesky | solution.py:24
  231.9 9.8 custom-call.15
  241.7 2.3 fusion.6
  244.9 4.0 convolution_subtract_fusion.5
  252.2 1.4 compare_reduce_fusion.10
  255.3 118.1 %all-gather.18.cloned.1.call-done = f32[2048,2048]{0,1:T(8,128)} async-done(((f32[128,2048]{0,1:T(8,128)}), f32[2048,2048]{0,1:T(8,128)}) %all-gather.18.cloned.1.call-update) | async-done | bytes 16777232 | tf_op jit(solution)/shard_map/all_gather | solution.py:55
  373.4 17.6 %copy.19 = f32[2048,2048]{1,0:T(8,128)} copy(f32[2048,2048]{0,1:T(8,128)} %all-gather.18.cloned.1.call-done) | data formatting | bytes 33554432 | tf_op jit(solution)/shard_map/all_gather | solution.py:55
  391.0 7.3 gather_fusion
  400.7 1.4 copy.20
  402.1 1.3 bitcast_add_fusion.1
  403.6 2.6 collective-permute-done
  407.0 47.7 %all-gather.20.cloned.1.call-done = f32[2048,128]{0,1:T(8,128)} async-done(((f32[128,128]{0,1:T(8,128)}), f32[2048,128]{0,1:T(8,128)}) %all-gather.20.cloned.1.call-update) | async-done | bytes 1048592 | tf_op jit(solution)/shard_map/all_gather | solution.py:22
  456.5 11.7 %cholesky.182 = f32[128,128]{1,0:T(8,128)S(1)} custom-call(f32[128,128]{1,0:T(8,128)S(1)} %fusion.23), custom_call_target="Cholesky" | custom-call | tf_op jit(solution)/shard_map/jit(cholesky)/cholesky | solution.py:24
  470.2 9.8 custom-call.16
  480.0 2.3 fusion.5
  482.3 1.8 convolution_subtract_fusion.4
  486.0 47.4 %all-gather.22.cloned.1.call-done = f32[2048,128]{0,1:T(8,128)} async-done(((f32[128,128]{0,1:T(8,128)}), f32[2048,128]{0,1:T(8,128)}) %all-gather.22.cloned.1.call-update) | async-done | bytes 1048592 | tf_op jit(solution)/shard_map/all_gather | solution.py:22
  535.2 11.7 %cholesky.193 = f32[128,128]{1,0:T(8,128)S(1)} custom-call(f32[128,128]{1,0:T(8,128)S(1)} %fusion.21), custom_call_target="Cholesky" | custom-call | tf_op jit(solution)/shard_map/jit(cholesky)/cholesky | solution.py:24
  548.9 9.8 custom-call.17
  558.7 2.3 fusion.4
  562.0 3.0 convolution_subtract_fusion.3
  566.1 47.2 %all-gather.24.cloned.1.call-done = f32[2048,128]{0,1:T(8,128)} async-done(((f32[128,128]{0,1:T(8,128)}), f32[2048,128]{0,1:T(8,128)}) %all-gather.24.cloned.1.call-update) | async-done | bytes 1048592 | tf_op jit(solution)/shard_map/all_gather | solution.py:22
  615.2 11.7 %cholesky.204 = f32[128,128]{1,0:T(8,128)S(1)} custom-call(f32[128,128]{1,0:T(8,128)S(1)} %fusion.19), custom_call_target="Cholesky" | custom-call | tf_op jit(solution)/shard_map/jit(cholesky)/cholesky | solution.py:24
  628.8 9.8 custom-call.18
  638.7 2.3 fusion.3
  641.9 2.8 convolution_subtract_fusion.2
  650.6 118.5 %all-gather.26.cloned.1.call-done = f32[2048,2048]{0,1:T(8,128)} async-done(((f32[128,2048]{0,1:T(8,128)}), f32[2048,2048]{0,1:T(8,128)}) %all-gather.26.cloned.1.call-update) | async-done | bytes 16777232 | tf_op jit(solution)/shard_map/all_gather | solution.py:55
  769.2 17.6 %copy.31 = f32[2048,2048]{1,0:T(8,128)} copy(f32[2048,2048]{0,1:T(8,128)} %all-gather.26.cloned.1.call-done) | data formatting | bytes 33554432 | tf_op jit(solution)/shard_map/all_gather | solution.py:55
  786.8 7.3 gather_fusion.1
  796.5 1.4 copy.32
  797.9 1.3 bitcast_add_fusion
  799.3 1.6 collective-permute-start.2
  800.9 22.0 %collective-permute-done.2 = f32[128,2048]{0,1:T(8,128)S(1)} collective-permute-done((f32[128,2048]{0,1:T(8,128)S(1)}, f32[128,2048]{0,1:T(8,128)S(1)}, u32[]{:S(2)}, u32[]{:S(2)}) %collective-permute-start.2) | collective-permute-done | bytes 1048608 | tf_op jit(solution)/shard_map/ppermute | solution.py:14
  823.7 47.7 %all-gather.28.cloned.1.call-done = f32[2048,128]{0,1:T(8,128)} async-done(((f32[128,128]{0,1:T(8,128)}), f32[2048,128]{0,1:T(8,128)}) %all-gather.28.cloned.1.call-update) | async-done | bytes 1048592 | tf_op jit(solution)/shard_map/all_gather | solution.py:22
  871.4 1.5 slice.252
  872.9 1.6 copy.35
  874.4 1.5 fusion.17
  875.9 13.2 %cholesky.215 = f32[128,128]{1,0:T(8,128)} custom-call(f32[128,128]{1,0:T(8,128)} %fusion.17), custom_call_target="Cholesky" | custom-call | tf_op jit(solution)/shard_map/jit(cholesky)/cholesky | solution.py:24
  890.6 2.2 select_bitcast_fusion.2
  892.8 11.3 %custom-call.19 = f32[1,128,128]{1,2,0:T(8,128)} custom-call(f32[1,128,128]{2,1,0:T(8,128)} %get-tuple-element.123), custom_call_target="InvertDiagBlocksLowerTriangular" | custom-call | tf_op jit(solution)/shard_map/triangular_solve/custom-call.0 | solution.py:25
  904.1 2.3 fusion.2
  906.4 1.8 convolution_subtract_fusion.1
  910.9 46.7 %all-gather.30.cloned.1.call-done = f32[2048,128]{0,1:T(8,128)} async-done(((f32[128,128]{0,1:T(8,128)}), f32[2048,128]{0,1:T(8,128)}) %all-gather.30.cloned.1.call-update) | async-done | bytes 1048592 | tf_op jit(solution)/shard_map/all_gather | solution.py:22
  959.4 11.7 %cholesky.226 = f32[128,128]{1,0:T(8,128)S(1)} custom-call(f32[128,128]{1,0:T(8,128)S(1)} %fusion.15), custom_call_target="Cholesky" | custom-call | tf_op jit(solution)/shard_map/jit(cholesky)/cholesky | solution.py:24
  972.5 10.4 custom-call.20
  982.9 2.3 fusion.1
  985.2 3.0 convolution_subtract_fusion
  1003.0 34.7 %all-gather.32.cloned.1.call-done = f32[2048,128]{0,1:T(8,128)} async-done(((f32[128,128]{0,1:T(8,128)}), f32[2048,128]{0,1:T(8,128)}) %all-gather.32.cloned.1.call-update) | async-done | bytes 1048592 | tf_op jit(solution)/shard_map/all_gather | solution.py:22
  1039.4 11.9 %cholesky.237 = f32[128,128]{1,0:T(8,128)S(1)} custom-call(f32[128,128]{1,0:T(8,128)S(1)} %fusion.13), custom_call_target="Cholesky" | custom-call | tf_op jit(solution)/shard_map/jit(cholesky)/cholesky | solution.py:24
  1052.7 9.8 custom-call.21
  1062.5 2.3 fusion
  1064.8 1.8 fusion.31
  1067.6 1.3 fusion.11
  (172 shorter events, 74.6 us)
Async XLA Ops:
  7.2 639.0 %copy-start = (s32[8,13]{1,0:T(8,128)S(1)}, s32[8,13]{1,0:T(8,128)}, u32[]{:S(2)}) copy-start(s32[8,13]{1,0:T(8,128)} %param.32) | copy-start | bytes 1252
  7.2 242.1 %copy-start.13 = (s32[1,13]{1,0:T(1,128)S(1)}, s32[1,13]{1,0:T(1,128)}, u32[]{:S(2)}) copy-start(s32[1,13]{1,0:T(1,128)} %param.31) | copy-start | bytes 160
  7.2 54.6 %all-gather.12.cloned.1.call-start = ((), (), s32[]{:S(2)}) async-start(), calls=%async_computation | async-start | bytes 1114112 | tf_op jit(solution)/shard_map/all_gather | solution.py:22
  9.2 129.7 %all-gather.14.cloned.1.call-start = ((), (), s32[]{:S(2)}) async-start(), calls=%async_computation.1 | async-start | bytes 1114112 | tf_op jit(solution)/shard_map/all_gather | solution.py:22
  91.2 125.8 %all-gather.16.cloned.1.call-start = ((), (), s32[]{:S(2)}) async-start(), calls=%async_computation.2 | async-start | bytes 1114112 | tf_op jit(solution)/shard_map/all_gather | solution.py:22
  167.7 1.0 copy-start.7
  169.3 204.1 %all-gather.18.cloned.1.call-start = ((), (), s32[]{:S(2)}) async-start(), calls=%async_computation.3 | async-start | bytes 17825792 | tf_op jit(solution)/shard_map/all_gather | solution.py:55
  243.9 1.0 copy-start.1
  249.0 205.7 %all-gather.20.cloned.1.call-start = ((), (), s32[]{:S(2)}) async-start(), calls=%async_computation.4 | async-start | bytes 1114112 | tf_op jit(solution)/shard_map/all_gather | solution.py:22
  403.5 2.7 collective-permute-start
  407.0 126.4 %all-gather.22.cloned.1.call-start = ((), (), s32[]{:S(2)}) async-start(), calls=%async_computation.5 | async-start | bytes 1114112 | tf_op jit(solution)/shard_map/all_gather | solution.py:22
  482.2 1.8 copy-start.2
  484.1 1.0 copy-start.8
  485.7 127.6 %all-gather.24.cloned.1.call-start = ((), (), s32[]{:S(2)}) async-start(), calls=%async_computation.6 | async-start | bytes 1114112 | tf_op jit(solution)/shard_map/all_gather | solution.py:22
  561.0 1.0 copy-start.3
  565.7 203.5 %all-gather.26.cloned.1.call-start = ((), (), s32[]{:S(2)}) async-start(), calls=%async_computation.7 | async-start | bytes 17825792 | tf_op jit(solution)/shard_map/all_gather | solution.py:55
  640.9 1.0 copy-start.4
  644.8 226.6 %all-gather.28.cloned.1.call-start = ((), (), s32[]{:S(2)}) async-start(), calls=%async_computation.8 | async-start | bytes 1114112 | tf_op jit(solution)/shard_map/all_gather | solution.py:22
  645.9 4.7 collective-permute-start.1
  799.2 195.6 %copy-start.10 = (f32[128,128]{1,0:T(8,128)S(1)}, f32[128,128]{1,0:T(8,128)}, u32[]{:S(2)}) copy-start(f32[128,128]{1,0:T(8,128)} %get-tuple-element.130) | copy-start | bytes 196612
  799.3 197.1 %copy-start.11 = (f32[128,128]{1,0:T(8,128)S(1)}, f32[128,128]{1,0:T(8,128)}, u32[]{:S(2)}) copy-start(f32[128,128]{1,0:T(8,128)} %get-tuple-element.128) | copy-start | bytes 196612
  799.3 198.7 %copy-start.12 = (f32[128,128]{1,0:T(8,128)S(1)}, f32[128,128]{1,0:T(8,128)}, u32[]{:S(2)}) copy-start(f32[128,128]{1,0:T(8,128)} %get-tuple-element.126) | copy-start | bytes 196612
  799.3 23.6 %collective-permute-start.2 = (f32[128,2048]{0,1:T(8,128)S(1)}, f32[128,2048]{0,1:T(8,128)S(1)}, u32[]{:S(2)}, u32[]{:S(2)}) collective-permute-start(f32[128,2048]{0,1:T(8,128)S(1)} %bitcast_add_fusion), channel_id=1, source_target_pairs={{0,32},{16,48},{32,0},{48,16},{64,96},{80,112},{96,64},{112,80},{1... | collective-permute-start | bytes 3145736 | tf_op jit(solution)/shard_map/ppermute | solution.py:14
  823.7 133.9 %all-gather.30.cloned.1.call-start = ((), (), s32[]{:S(2)}) async-start(), calls=%async_computation.9 | async-start | bytes 1114112 | tf_op jit(solution)/shard_map/all_gather | solution.py:22
  906.4 1.8 copy-start.5
  908.2 1.0 copy-start.6
  909.9 127.7 %all-gather.32.cloned.1.call-start = ((), (), s32[]{:S(2)}) async-start(), calls=%async_computation.10 | async-start | bytes 1114112 | tf_op jit(solution)/shard_map/all_gather | solution.py:22
  988.2 1.0 copy-start.9
Sparse Core Ops, SparseCore 0:
  11.0 50.7 all-gather.11
  91.3 47.5 all-gather.13
  169.4 47.5 all-gather.15
  249.1 124.2 all-gather.17
  407.1 47.5 all-gather.19
  485.9 47.5 all-gather.21
  565.8 47.5 all-gather.23
  644.9 124.2 all-gather.25
  823.8 47.5 all-gather.27
  910.0 47.5 all-gather.29
  990.1 47.5 all-gather.31
where the time goes:
time: 1090 us; the launch traced here: 1080 us
  waiting for transfers between devices  680 us (62%)
  other arithmetic  237 us (22%)
  local copies, waits for them, and re-layouts  94.7 us (9%)
  matrix products  44.9 us (4%)
  between operations  16.4 us (2%)
    all_gather x9, waiting for transfers between devices, eliminate(): lax.all_gather(front[:, block_low:block_low + BLK], 'fr', axis=0, tiled=T...  419 us
    all_gather x2, waiting for transfers between devices, extend(): shard_rows = lax.all_gather(front, 'fr', axis=0, tiled=True)  237 us
    another operation x27, other arithmetic, eliminate(): lower_block = jnp.linalg.cholesky(gathered[block_low:block_low + BLK])  114 us
    another operation x18, other arithmetic, eliminate(): lax.linalg.triangular_solve(lower_block, gathered, left_side=False, lower...  99.7 us
    all_gather x2, local copies, waits for them, and re-layouts, extend(): shard_rows = lax.all_gather(front, 'fr', axis=0, tiled=True)  35.2 us
    ppermute x3, waiting for transfers between devices, partner(): lax.ppermute(array, axis, [(i, i ^ 1 << stride) for i in range(lax.axis_s...  24.6 us
    dot_general x9, matrix products, eliminate(): jnp.dot(own_below, below.T, precision=HIGH, preferred_element_type=jnp.fl...  22 us
  transfers between devices with their start and end apart: 14, of which 13 were waited for; matrix products, arithmetic and copies ran while one was open for 2% of the time, Pallas kernels for 0%

commit v1 on v0

--- a/solution.py
+++ b/solution.py
@@ -1,3 +1,4 @@
+import functools
 import jax
 import jax.numpy as jnp
 from jax import lax
@@ -8,6 +9,33 @@
 NFB = 16
 NPB = 3
 HIGH = lax.Precision.HIGHEST
+
+
+def do_column_for(local_x, comm_axis):
+    k_now = jax.lax.axis_size(comm_axis)
+    field_out, block_next, arr_next = (k_now, jax.lax.axis_index(comm_axis), local_x.shape[0])
+    main = tuple((k0 * field_out if w == 0 else k0 for w, k0 in enumerate(local_x.shape)))
+    reached = lax.dynamic_update_slice_in_dim(
+        jnp.zeros(main, local_x.dtype), local_x, block_next * arr_next, axis=0
+    )
+    item_now = inter = local_x
+    for dev in tuple(range(1, field_out // 2 + 1)):
+        z2 = tuple(((w, (w + 1) % field_out) for w in range(field_out)))
+        item_now = jax.lax.ppermute(item_now, axis_name=comm_axis, perm=z2)
+        reached = lax.dynamic_update_slice_in_dim(
+            reached, item_now, (block_next - dev) % field_out * arr_next, axis=0
+        )
+        if 2 * dev < field_out:
+            inter = jax.lax.ppermute(
+                inter, comm_axis, tuple(((w, (w - 1) % field_out) for w in range(field_out)))
+            )
+            reached = lax.dynamic_update_slice_in_dim(
+                reached, inter, (block_next + dev) % field_out * arr_next, axis=0
+            )
+    return reached
+
+
+fill_the_tails = functools.partial(do_column_for, comm_axis="fr")
 
 
 def partner(array, axis, stride):
@@ -52,7 +80,7 @@
     source_block = jnp.sum(jnp.where(matches, jnp.arange(NFB)[None, :], 0), axis=1)
     source_rows = (source_block[:, None] * BLK + jnp.arange(BLK)[None, :]).reshape(row_count)
     is_live = jnp.repeat(present, BLK)
-    shard_rows = lax.all_gather(front, "fr", axis=0, tiled=True)
+    shard_rows = fill_the_tails(front)
     inside = is_live & (source_rows >= 0) & (source_rows < shard_rows.shape[0])
     picked_rows = jnp.take(shard_rows, jnp.clip(source_rows, 0, shard_rows.shape[0] - 1), axis=0)
     picked_rows = jnp.where(inside[:, None], picked_rows, 0.0)

time: 1090 us -> 1200 us (1.10)
  local copies, waits for them, and re-layouts: 94.7 us -> 182 us
  starting transfers between devices: 4.07 us -> 65.1 us
  waiting for transfers between devices: 680 us -> 640 us
    all_gather x2 -> x0, waiting for transfers between devices: 237 us -> none  [extend(): shard_rows = lax.all_gather(front, 'fr', axis=0, tiled=True)]
    ppermute x0 -> x30, waiting for transfers between devices: none -> 201 us  [the longest x16 194 us: do_column_for(): item_now = jax.lax.ppermute(item_now, axis_name=comm_axis, perm=z2)]
    ppermute x0 -> x30, starting transfers between devices: none -> 61 us  [the longest x14 59.2 us: do_column_for(): jax.lax.ppermute(inter, comm_axis, tuple(((w, (w - 1) % field_out) for w...]
    ppermute x0 -> x30, local copies, waits for them, and re-layouts: none -> 56.8 us  [the longest x16 31 us: do_column_for(): item_now = jax.lax.ppermute(item_now, axis_name=comm_axis, perm=z2)]
    dynamic_update_slice x0 -> x32, local copies, waits for them, and re-layouts: none -> 46.8 us  [the longest x16 24.6 us: do_column_for(): lax.dynamic_update_slice_in_dim(reached, item_now, (block_next - dev) % f...]
    all_gather x2 -> x0, local copies, waits for them, and re-layouts: 35.2 us -> none  [extend(): shard_rows = lax.all_gather(front, 'fr', axis=0, tiled=True)]
    another operation x0 -> x2, local copies, waits for them, and re-layouts: none -> 15.8 us
  transfers between devices with their start and end apart: 14 -> 42, of which waited for: 13 -> 27; matrix products, arithmetic and copies ran while one was open for 2% -> 12% of each run, Pallas kernels for 0% -> 0%
where the time goes in v1:
time: 1200 us; the launch traced here: 1180 us
  waiting for transfers between devices  640 us (53%)
  other arithmetic  238 us (20%)
  local copies, waits for them, and re-layouts  182 us (15%)
  starting transfers between devices  65.1 us (5%)
  matrix products  42.3 us (4%)
  between operations  17.1 us (1%)
    all_gather x9, waiting for transfers between devices, eliminate(): lax.all_gather(front[:, block_low:block_low + BLK], 'fr', axis=0, tiled=T...  422 us
    ppermute x16, waiting for transfers between devices, do_column_for(): item_now = jax.lax.ppermute(item_now, axis_name=comm_axis, perm=z2)  194 us
    another operation x27, other arithmetic, eliminate(): lower_block = jnp.linalg.cholesky(gathered[block_low:block_low + BLK])  114 us
    another operation x18, other arithmetic, eliminate(): lax.linalg.triangular_solve(lower_block, gathered, left_side=False, lower...  101 us
    ppermute x14, starting transfers between devices, do_column_for(): jax.lax.ppermute(inter, comm_axis, tuple(((w, (w - 1) % field_out) for w...  59.2 us
    ppermute x16, local copies, waits for them, and re-layouts, do_column_for(): item_now = jax.lax.ppermute(item_now, axis_name=comm_axis, perm=z2)  31 us
    ppermute x14, local copies, waits for them, and re-layouts, do_column_for(): jax.lax.ppermute(inter, comm_axis, tuple(((w, (w - 1) % field_out) for w...  25.8 us
    dynamic_update_slice x16, local copies, waits for them, and re-layouts, do_column_for(): lax.dynamic_update_slice_in_dim(reached, item_now, (block_next - dev) % f...  24.6 us
  transfers between devices with their start and end apart: 42, of which 27 were waited for; matrix products, arithmetic and copies ran while one was open for 12% of the time, Pallas kernels for 0%

profile of v1, /device:TPU:2, one launch (start us, length us, event | category | flops | bytes accessed | tf_op | source)
XLA Modules:
  0.0 1184.9 jit_solution(18114673090374898388)
XLA Ops:
  9.3 52.5 %all-gather.10.cloned.1.call-done = f32[2048,128]{0,1:T(8,128)} async-done(((f32[128,128]{0,1:T(8,128)}), f32[2048,128]{0,1:T(8,128)}) %all-gather.10.cloned.1.call-update) | async-done | bytes 1048592 | tf_op jit(solution)/shard_map/all_gather | solution.py:50
  63.6 11.7 cholesky.149
  77.3 9.8 custom-call.13
  92.1 47.4 %all-gather.12.cloned.1.call-done = f32[2048,128]{0,1:T(8,128)} async-done(((f32[128,128]{0,1:T(8,128)}), f32[2048,128]{0,1:T(8,128)}) %all-gather.12.cloned.1.call-update) | async-done | bytes 1048592 | tf_op jit(solution)/shard_map/all_gather | solution.py:50
  141.3 11.7 cholesky.160
  155.0 9.8 custom-call.14
  171.0 47.2 %all-gather.14.cloned.1.call-done = f32[2048,128]{0,1:T(8,128)} async-done(((f32[128,128]{0,1:T(8,128)}), f32[2048,128]{0,1:T(8,128)}) %all-gather.14.cloned.1.call-update) | async-done | bytes 1048592 | tf_op jit(solution)/shard_map/all_gather | solution.py:50
  220.0 11.7 cholesky.171
  233.7 9.8 custom-call.15
  246.8 3.0 convolution_subtract_fusion.5
  251.9 21.3 %collective-permute-done = f32[128,2048]{0,1:T(8,128)S(1)} collective-permute-done((f32[128,2048]{0,1:T(8,128)S(1)}, f32[128,2048]{0,1:T(8,128)S(1)}, u32[]{:S(2)}, u32[]{:S(2)}) %collective-permute-start) | collective-permute-done | bytes 1048608 | tf_op jit(solution)/shard_map/ppermute | solution.py:24
  274.1 3.3 collective-permute-start.3
  277.5 20.6 %collective-permute-done.2 = f32[128,2048]{0,1:T(8,128)S(1)} collective-permute-done((f32[128,2048]{0,1:T(8,128)S(1)}, f32[128,2048]{0,1:T(8,128)S(1)}, u32[]{:S(2)}, u32[]{:S(2)}) %collective-permute-start.2) | collective-permute-done | bytes 1048608 | tf_op jit(solution)/shard_map/ppermute | solution.py:24
  298.2 5.1 collective-permute-start.5
  303.4 19.7 %collective-permute-done.4 = f32[128,2048]{0,1:T(8,128)S(1)} collective-permute-done((f32[128,2048]{0,1:T(8,128)S(1)}, f32[128,2048]{0,1:T(8,128)S(1)}, u32[]{:S(2)}, u32[]{:S(2)}) %collective-permute-start.4) | collective-permute-done | bytes 1048608 | tf_op jit(solution)/shard_map/ppermute | solution.py:24
  323.1 5.1 collective-permute-start.7
  328.3 19.0 %collective-permute-done.6 = f32[128,2048]{0,1:T(8,128)} collective-permute-done((f32[128,2048]{0,1:T(8,128)S(1)}, f32[128,2048]{0,1:T(8,128)}, u32[]{:S(2)}, u32[]{:S(2)}) %collective-permute-start.6) | collective-permute-done | bytes 1048608 | tf_op jit(solution)/shard_map/ppermute | solution.py:24
  351.1 5.1 collective-permute-start.9
  358.3 12.4 %collective-permute-done.8 = f32[128,2048]{0,1:T(8,128)} collective-permute-done((f32[128,2048]{0,1:T(8,128)}, f32[128,2048]{0,1:T(8,128)}, u32[]{:S(2)}, u32[]{:S(2)}) %collective-permute-start.8) | collective-permute-done | bytes 1048608 | tf_op jit(solution)/shard_map/ppermute | solution.py:24
  370.7 7.9 broadcast.263.clone
  388.7 5.1 collective-permute-start.11
  409.4 2.8 collective-permute-done.11
  412.2 4.5 collective-permute-start.13
  417.8 2.6 copy.28
  440.5 5.1 collective-permute-done.14
  448.2 7.2 gather_fusion
  459.3 2.6 collective-permute-done.15
  463.0 49.2 %all-gather.16.cloned.1.call-done = f32[2048,128]{0,1:T(8,128)} async-done(((f32[128,128]{0,1:T(8,128)}), f32[2048,128]{0,1:T(8,128)}) %all-gather.16.cloned.1.call-update) | async-done | bytes 1048592 | tf_op jit(solution)/shard_map/all_gather | solution.py:50
  514.0 11.7 cholesky.182
  527.8 9.8 custom-call.16
  543.8 47.2 %all-gather.18.cloned.1.call-done = f32[2048,128]{0,1:T(8,128)} async-done(((f32[128,128]{0,1:T(8,128)}), f32[2048,128]{0,1:T(8,128)}) %all-gather.18.cloned.1.call-update) | async-done | bytes 1048592 | tf_op jit(solution)/shard_map/all_gather | solution.py:50
  592.8 11.7 cholesky.193
  606.4 9.8 custom-call.17
  619.5 3.0 convolution_subtract_fusion.3
  623.4 47.5 %all-gather.20.cloned.1.call-done = f32[2048,128]{0,1:T(8,128)} async-done(((f32[128,128]{0,1:T(8,128)}), f32[2048,128]{0,1:T(8,128)}) %all-gather.20.cloned.1.call-update) | async-done | bytes 1048592 | tf_op jit(solution)/shard_map/all_gather | solution.py:50
  672.7 11.7 cholesky.204
  686.4 9.8 custom-call.18
  703.4 21.3 %collective-permute-done.16 = f32[128,2048]{0,1:T(8,128)S(1)} collective-permute-done((f32[128,2048]{0,1:T(8,128)S(1)}, f32[128,2048]{0,1:T(8,128)S(1)}, u32[]{:S(2)}, u32[]{:S(2)}) %collective-permute-start.16) | collective-permute-done | bytes 1048608 | tf_op jit(solution)/shard_map/ppermute | solution.py:24
  725.6 3.3 collective-permute-start.19
  728.9 20.6 %collective-permute-done.18 = f32[128,2048]{0,1:T(8,128)S(1)} collective-permute-done((f32[128,2048]{0,1:T(8,128)S(1)}, f32[128,2048]{0,1:T(8,128)S(1)}, u32[]{:S(2)}, u32[]{:S(2)}) %collective-permute-start.18) | collective-permute-done | bytes 1048608 | tf_op jit(solution)/shard_map/ppermute | solution.py:24
  749.7 5.1 collective-permute-start.21
  754.9 19.7 %collective-permute-done.20 = f32[128,2048]{0,1:T(8,128)S(1)} collective-permute-done((f32[128,2048]{0,1:T(8,128)S(1)}, f32[128,2048]{0,1:T(8,128)S(1)}, u32[]{:S(2)}, u32[]{:S(2)}) %collective-permute-start.20) | collective-permute-done | bytes 1048608 | tf_op jit(solution)/shard_map/ppermute | solution.py:24
  774.6 5.1 collective-permute-start.23
  779.7 19.0 %collective-permute-done.22 = f32[128,2048]{0,1:T(8,128)} collective-permute-done((f32[128,2048]{0,1:T(8,128)S(1)}, f32[128,2048]{0,1:T(8,128)}, u32[]{:S(2)}, u32[]{:S(2)}) %collective-permute-start.22) | collective-permute-done | bytes 1048608 | tf_op jit(solution)/shard_map/ppermute | solution.py:24
  802.6 5.1 collective-permute-start.25
  812.0 10.2 collective-permute-done.24
  822.2 7.9 broadcast.263
  840.2 5.1 collective-permute-start.27
  860.9 2.6 collective-permute-done.27
  863.5 4.7 collective-permute-start.29
  869.3 2.6 copy.55
  892.0 5.3 collective-permute-done.30
  899.9 7.4 gather_fusion.1
  914.2 14.8 %collective-permute-done.32 = f32[128,2048]{0,1:T(8,128)S(1)} collective-permute-done((f32[128,2048]{0,1:T(8,128)S(1)}, f32[128,2048]{0,1:T(8,128)S(1)}, u32[]{:S(2)}, u32[]{:S(2)}) %collective-permute-start.32) | collective-permute-done | bytes 1048608 | tf_op jit(solution)/shard_map/ppermute | solution.py:42
  929.9 49.4 %all-gather.22.cloned.1.call-done = f32[2048,128]{0,1:T(8,128)} async-done(((f32[128,128]{0,1:T(8,128)}), f32[2048,128]{0,1:T(8,128)}) %all-gather.22.cloned.1.call-update) | async-done | bytes 1048592 | tf_op jit(solution)/shard_map/all_gather | solution.py:50
  983.9 13.2 %cholesky.215 = f32[128,128]{1,0:T(8,128)} custom-call(f32[128,128]{1,0:T(8,128)} %fusion.17), custom_call_target="Cholesky" | custom-call | tf_op jit(solution)/shard_map/jit(cholesky)/cholesky | solution.py:52
  1000.8 11.3 custom-call.19
  1018.8 46.7 %all-gather.24.cloned.1.call-done = f32[2048,128]{0,1:T(8,128)} async-done(((f32[128,128]{0,1:T(8,128)}), f32[2048,128]{0,1:T(8,128)}) %all-gather.24.cloned.1.call-update) | async-done | bytes 1048592 | tf_op jit(solution)/shard_map/all_gather | solution.py:50
  1067.3 11.7 cholesky.226
  1080.3 10.4 custom-call.20
  1093.0 3.0 convolution_subtract_fusion
  1110.8 34.6 %all-gather.26.cloned.1.call-done = f32[2048,128]{0,1:T(8,128)} async-done(((f32[128,128]{0,1:T(8,128)}), f32[2048,128]{0,1:T(8,128)}) %all-gather.26.cloned.1.call-update) | async-done | bytes 1048592 | tf_op jit(solution)/shard_map/all_gather | solution.py:50
  1147.2 12.0 %cholesky.237 = f32[128,128]{1,0:T(8,128)S(1)} custom-call(f32[128,128]{1,0:T(8,128)S(1)} %fusion.13), custom_call_target="Cholesky" | custom-call | tf_op jit(solution)/shard_map/jit(cholesky)/cholesky | solution.py:52
  1160.5 9.8 custom-call.21
  (328 shorter events, 230.1 us)
Async XLA Ops:
  7.2 792.7 %copy-start = (s32[8,13]{1,0:T(8,128)S(1)}, s32[8,13]{1,0:T(8,128)}, u32[]{:S(2)}) copy-start(s32[8,13]{1,0:T(8,128)} %param.32) | copy-start | bytes 1252
  7.2 340.3 %copy-start.32 = (s32[1,13]{1,0:T(1,128)S(1)}, s32[1,13]{1,0:T(1,128)}, u32[]{:S(2)}) copy-start(s32[1,13]{1,0:T(1,128)} %param.31) | copy-start | bytes 160
  7.2 342.2 %copy-start.30 = (f32[128,384]{1,0:T(8,128)S(1)}, f32[128,384]{1,0:T(8,128)}, u32[]{:S(2)}) copy-start(f32[128,384]{1,0:T(8,128)} %param.29) | copy-start | bytes 589828
  7.2 54.6 %all-gather.10.cloned.1.call-start = ((), (), s32[]{:S(2)}) async-start(), calls=%async_computation | async-start | bytes 1114112 | tf_op jit(solution)/shard_map/all_gather | solution.py:50
  9.3 130.3 %all-gather.12.cloned.1.call-start = ((), (), s32[]{:S(2)}) async-start(), calls=%async_computation.1 | async-start | bytes 1114112 | tf_op jit(solution)/shard_map/all_gather | solution.py:50
  91.8 126.4 %all-gather.14.cloned.1.call-start = ((), (), s32[]{:S(2)}) async-start(), calls=%async_computation.2 | async-start | bytes 1114112 | tf_op jit(solution)/shard_map/all_gather | solution.py:50
  170.5 341.7 %all-gather.16.cloned.1.call-start = ((), (), s32[]{:S(2)}) async-start(), calls=%async_computation.3 | async-start | bytes 1114112 | tf_op jit(solution)/shard_map/all_gather | solution.py:50
  249.8 23.4 %collective-permute-start = (f32[128,2048]{0,1:T(8,128)S(1)}, f32[128,2048]{0,1:T(8,128)S(1)}, u32[]{:S(2)}, u32[]{:S(2)}) collective-permute-start(f32[128,2048]{0,1:T(8,128)S(1)} %convolution_subtract_fusion.5), channel_id=1, source_target_pairs={{0,1},{1,2},{2,3},{3,4},{4,5},{5,6},{6,7},{7,8},{8,9},{9,10},{10,1... | collective-permute-start | bytes 3145736 | tf_op jit(solution)/shard_map/ppermute | solution.py:24
  250.8 23.3 %collective-permute-start.1 = (f32[128,2048]{0,1:T(8,128)S(1)}, f32[128,2048]{0,1:T(8,128)S(1)}, u32[]{:S(2)}, u32[]{:S(2)}) collective-permute-start(f32[128,2048]{0,1:T(8,128)S(1)} %convolution_subtract_fusion.5), channel_id=1, source_target_pairs={{0,15},{1,0},{2,1},{3,2},{4,3},{5,4},{6,5},{7,6},{8,7},{9,8},{10,9... | collective-permute-start | bytes 3145736 | tf_op jit(solution)/shard_map/ppermute | solution.py:29
  273.2 4.3 copy-start.15
  273.2 24.9 %collective-permute-start.2 = (f32[128,2048]{0,1:T(8,128)S(1)}, f32[128,2048]{0,1:T(8,128)S(1)}, u32[]{:S(2)}, u32[]{:S(2)}) collective-permute-start(f32[128,2048]{0,1:T(8,128)S(1)} %collective-permute-done), channel_id=1, source_target_pairs={{0,1},{1,2},{2,3},{3,4},{4,5},{5,6},{6,7},{7,8},{8,9},{9,10},{10,1... | collective-permute-start | bytes 3145736 | tf_op jit(solution)/shard_map/ppermute | solution.py:24
  274.1 73.1 %copy-start.17 = (f32[128,2048]{0,1:T(8,128)}, f32[128,2048]{0,1:T(8,128)S(1)}, u32[]{:S(2)}) copy-start(f32[128,2048]{0,1:T(8,128)S(1)} %collective-permute-done.1) | copy-start | bytes 3145732
  274.1 24.1 %collective-permute-start.3 = (f32[128,2048]{0,1:T(8,128)S(1)}, f32[128,2048]{0,1:T(8,128)S(1)}, u32[]{:S(2)}, u32[]{:S(2)}) collective-permute-start(f32[128,2048]{0,1:T(8,128)S(1)} %collective-permute-done.1), channel_id=1, source_target_pairs={{0,15},{1,0},{2,1},{3,2},{4,3},{5,4},{6,5},{7,6},{8,7},{9,8},{10,9... | collective-permute-start | bytes 3145736 | tf_op jit(solution)/shard_map/ppermute | solution.py:29
  298.0 49.2 %copy-start.16 = (f32[128,2048]{0,1:T(8,128)}, f32[128,2048]{0,1:T(8,128)S(1)}, u32[]{:S(2)}) copy-start(f32[128,2048]{0,1:T(8,128)S(1)} %collective-permute-done.2) | copy-start | bytes 3145732
  298.0 25.0 %collective-permute-start.4 = (f32[128,2048]{0,1:T(8,128)S(1)}, f32[128,2048]{0,1:T(8,128)S(1)}, u32[]{:S(2)}, u32[]{:S(2)}) collective-permute-start(f32[128,2048]{0,1:T(8,128)S(1)} %collective-permute-done.2), channel_id=1, source_target_pairs={{0,1},{1,2},{2,3},{3,4},{4,5},{5,6},{6,7},{7,8},{8,9},{9,10},{10,1... | collective-permute-start | bytes 3145736 | tf_op jit(solution)/shard_map/ppermute | solution.py:24
  298.2 24.9 %copy-start.13 = (f32[128,2048]{0,1:T(8,128)}, f32[128,2048]{0,1:T(8,128)S(1)}, u32[]{:S(2)}) copy-start(f32[128,2048]{0,1:T(8,128)S(1)} %collective-permute-done.3) | copy-start | bytes 3145732
  298.2 24.9 %collective-permute-start.5 = (f32[128,2048]{0,1:T(8,128)S(1)}, f32[128,2048]{0,1:T(8,128)S(1)}, u32[]{:S(2)}, u32[]{:S(2)}) collective-permute-start(f32[128,2048]{0,1:T(8,128)S(1)} %collective-permute-done.3), channel_id=1, source_target_pairs={{0,15},{1,0},{2,1},{3,2},{4,3},{5,4},{6,5},{7,6},{8,7},{9,8},{10,9... | collective-permute-start | bytes 3145736 | tf_op jit(solution)/shard_map/ppermute | solution.py:29
  323.1 5.2 copy-start.14
  323.1 24.1 %collective-permute-start.6 = (f32[128,2048]{0,1:T(8,128)S(1)}, f32[128,2048]{0,1:T(8,128)}, u32[]{:S(2)}, u32[]{:S(2)}) collective-permute-start(f32[128,2048]{0,1:T(8,128)S(1)} %collective-permute-done.4), channel_id=1, source_target_pairs={{0,1},{1,2},{2,3},{3,4},{4,5},{5,6},{6,7},{7,8},{8,9},{9,10},{10,1... | collective-permute-start | bytes 3145736 | tf_op jit(solution)/shard_map/ppermute | solution.py:24
  323.1 33.6 %copy-start.12 = (f32[128,2048]{0,1:T(8,128)}, f32[128,2048]{0,1:T(8,128)S(1)}, u32[]{:S(2)}) copy-start(f32[128,2048]{0,1:T(8,128)S(1)} %collective-permute-done.5) | copy-start | bytes 3145732
  323.1 27.9 %collective-permute-start.7 = (f32[128,2048]{0,1:T(8,128)S(1)}, f32[128,2048]{0,1:T(8,128)}, u32[]{:S(2)}, u32[]{:S(2)}) collective-permute-start(f32[128,2048]{0,1:T(8,128)S(1)} %collective-permute-done.5), channel_id=1, source_target_pairs={{0,15},{1,0},{2,1},{3,2},{4,3},{5,4},{6,5},{7,6},{8,7},{9,8},{10,9... | collective-permute-start | bytes 3145736 | tf_op jit(solution)/shard_map/ppermute | solution.py:29
  347.2 23.5 %collective-permute-start.8 = (f32[128,2048]{0,1:T(8,128)}, f32[128,2048]{0,1:T(8,128)}, u32[]{:S(2)}, u32[]{:S(2)}) collective-permute-start(f32[128,2048]{0,1:T(8,128)} %collective-permute-done.6), channel_id=1, source_target_pairs={{0,1},{1,2},{2,3},{3,4},{4,5},{5,6},{6,7},{7,8},{8,9},{9,10},{10,1... | collective-permute-start | bytes 3145736 | tf_op jit(solution)/shard_map/ppermute | solution.py:24
  351.1 37.7 %collective-permute-start.9 = (f32[128,2048]{0,1:T(8,128)}, f32[128,2048]{0,1:T(8,128)}, u32[]{:S(2)}, u32[]{:S(2)}) collective-permute-start(f32[128,2048]{0,1:T(8,128)} %collective-permute-done.7), channel_id=1, source_target_pairs={{0,15},{1,0},{2,1},{3,2},{4,3},{5,4},{6,5},{7,6},{8,7},{9,8},{10,9... | collective-permute-start | bytes 3145736 | tf_op jit(solution)/shard_map/ppermute | solution.py:29
  370.7 28.4 %collective-permute-start.10 = (f32[128,2048]{0,1:T(8,128)}, f32[128,2048]{0,1:T(8,128)}, u32[]{:S(2)}, u32[]{:S(2)}) collective-permute-start(f32[128,2048]{0,1:T(8,128)} %collective-permute-done.8), channel_id=1, source_target_pairs={{0,1},{1,2},{2,3},{3,4},{4,5},{5,6},{6,7},{7,8},{8,9},{9,10},{10,1... | collective-permute-start | bytes 3145736 | tf_op jit(solution)/shard_map/ppermute | solution.py:24
  388.7 23.5 %collective-permute-start.11 = (f32[128,2048]{0,1:T(8,128)}, f32[128,2048]{0,1:T(8,128)}, u32[]{:S(2)}, u32[]{:S(2)}) collective-permute-start(f32[128,2048]{0,1:T(8,128)} %collective-permute-done.9), channel_id=1, source_target_pairs={{0,15},{1,0},{2,1},{3,2},{4,3},{5,4},{6,5},{7,6},{8,7},{9,8},{10,9... | collective-permute-start | bytes 3145736 | tf_op jit(solution)/shard_map/ppermute | solution.py:29
  399.2 25.2 %collective-permute-start.12 = (f32[128,2048]{0,1:T(8,128)}, f32[128,2048]{0,1:T(8,128)}, u32[]{:S(2)}, u32[]{:S(2)}) collective-permute-start(f32[128,2048]{0,1:T(8,128)} %collective-permute-done.10), channel_id=1, source_target_pairs={{0,1},{1,2},{2,3},{3,4},{4,5},{5,6},{6,7},{7,8},{8,9},{9,10},{10,1... | collective-permute-start | bytes 3145736 | tf_op jit(solution)/shard_map/ppermute | solution.py:24
  412.2 22.3 %collective-permute-start.13 = (f32[128,2048]{0,1:T(8,128)}, f32[128,2048]{0,1:T(8,128)}, u32[]{:S(2)}, u32[]{:S(2)}) collective-permute-start(f32[128,2048]{0,1:T(8,128)} %collective-permute-done.11), channel_id=1, source_target_pairs={{0,15},{1,0},{2,1},{3,2},{4,3},{5,4},{6,5},{7,6},{8,7},{9,8},{10,9... | collective-permute-start | bytes 3145736 | tf_op jit(solution)/shard_map/ppermute | solution.py:29
  424.3 21.3 %collective-permute-start.14 = (f32[128,2048]{0,1:T(8,128)}, f32[128,2048]{0,1:T(8,128)}, u32[]{:S(2)}, u32[]{:S(2)}) collective-permute-start(f32[128,2048]{0,1:T(8,128)} %collective-permute-done.12), channel_id=1, source_target_pairs={{0,1},{1,2},{2,3},{3,4},{4,5},{5,6},{6,7},{7,8},{8,9},{9,10},{10,1... | collective-permute-start | bytes 3145736 | tf_op jit(solution)/shard_map/ppermute | solution.py:24
  427.0 28.9 %copy-start.31 = (s32[16]{0:T(128)S(1)}, s32[16]{0:T(128)}, u32[]{:S(2)}) copy-start(s32[16]{0:T(128)} %get-tuple-element.139) | copy-start | bytes 196
  459.2 2.7 collective-permute-start.15
  462.7 128.3 %all-gather.18.cloned.1.call-start = ((), (), s32[]{:S(2)}) async-start(), calls=%async_computation.4 | async-start | bytes 1114112 | tf_op jit(solution)/shard_map/all_gather | solution.py:50
  543.3 127.5 %all-gather.20.cloned.1.call-start = ((), (), s32[]{:S(2)}) async-start(), calls=%async_computation.5 | async-start | bytes 1114112 | tf_op jit(solution)/shard_map/all_gather | solution.py:50
  623.2 356.2 %all-gather.22.cloned.1.call-start = ((), (), s32[]{:S(2)}) async-start(), calls=%async_computation.6 | async-start | bytes 1114112 | tf_op jit(solution)/shard_map/all_gather | solution.py:50
  701.3 23.4 %collective-permute-start.16 = (f32[128,2048]{0,1:T(8,128)S(1)}, f32[128,2048]{0,1:T(8,128)S(1)}, u32[]{:S(2)}, u32[]{:S(2)}) collective-permute-start(f32[128,2048]{0,1:T(8,128)S(1)} %convolution_subtract_fusion.2), channel_id=1, source_target_pairs={{0,1},{1,2},{2,3},{3,4},{4,5},{5,6},{6,7},{7,8},{8,9},{9,10},{10,1... | collective-permute-start | bytes 3145736 | tf_op jit(solution)/shard_map/ppermute | solution.py:24
  702.3 23.3 %collective-permute-start.17 = (f32[128,2048]{0,1:T(8,128)S(1)}, f32[128,2048]{0,1:T(8,128)S(1)}, u32[]{:S(2)}, u32[]{:S(2)}) collective-permute-start(f32[128,2048]{0,1:T(8,128)S(1)} %convolution_subtract_fusion.2), channel_id=1, source_target_pairs={{0,15},{1,0},{2,1},{3,2},{4,3},{5,4},{6,5},{7,6},{8,7},{9,8},{10,9... | collective-permute-start | bytes 3145736 | tf_op jit(solution)/shard_map/ppermute | solution.py:29
  724.6 4.3 copy-start.22
  724.6 24.9 %collective-permute-start.18 = (f32[128,2048]{0,1:T(8,128)S(1)}, f32[128,2048]{0,1:T(8,128)S(1)}, u32[]{:S(2)}, u32[]{:S(2)}) collective-permute-start(f32[128,2048]{0,1:T(8,128)S(1)} %collective-permute-done.16), channel_id=1, source_target_pairs={{0,1},{1,2},{2,3},{3,4},{4,5},{5,6},{6,7},{7,8},{8,9},{9,10},{10,1... | collective-permute-start | bytes 3145736 | tf_op jit(solution)/shard_map/ppermute | solution.py:24
  725.6 73.1 %copy-start.23 = (f32[128,2048]{0,1:T(8,128)}, f32[128,2048]{0,1:T(8,128)S(1)}, u32[]{:S(2)}) copy-start(f32[128,2048]{0,1:T(8,128)S(1)} %collective-permute-done.17) | copy-start | bytes 3145732
  725.6 24.1 %collective-permute-start.19 = (f32[128,2048]{0,1:T(8,128)S(1)}, f32[128,2048]{0,1:T(8,128)S(1)}, u32[]{:S(2)}, u32[]{:S(2)}) collective-permute-start(f32[128,2048]{0,1:T(8,128)S(1)} %collective-permute-done.17), channel_id=1, source_target_pairs={{0,15},{1,0},{2,1},{3,2},{4,3},{5,4},{6,5},{7,6},{8,7},{9,8},{10,9... | collective-permute-start | bytes 3145736 | tf_op jit(solution)/shard_map/ppermute | solution.py:29
  749.5 49.2 %copy-start.21 = (f32[128,2048]{0,1:T(8,128)}, f32[128,2048]{0,1:T(8,128)S(1)}, u32[]{:S(2)}) copy-start(f32[128,2048]{0,1:T(8,128)S(1)} %collective-permute-done.18) | copy-start | bytes 3145732
  749.5 25.1 %collective-permute-start.20 = (f32[128,2048]{0,1:T(8,128)S(1)}, f32[128,2048]{0,1:T(8,128)S(1)}, u32[]{:S(2)}, u32[]{:S(2)}) collective-permute-start(f32[128,2048]{0,1:T(8,128)S(1)} %collective-permute-done.18), channel_id=1, source_target_pairs={{0,1},{1,2},{2,3},{3,4},{4,5},{5,6},{6,7},{7,8},{8,9},{9,10},{10,1... | collective-permute-start | bytes 3145736 | tf_op jit(solution)/shard_map/ppermute | solution.py:24
  749.7 24.9 %copy-start.19 = (f32[128,2048]{0,1:T(8,128)}, f32[128,2048]{0,1:T(8,128)S(1)}, u32[]{:S(2)}) copy-start(f32[128,2048]{0,1:T(8,128)S(1)} %collective-permute-done.19) | copy-start | bytes 3145732
  749.7 24.9 %collective-permute-start.21 = (f32[128,2048]{0,1:T(8,128)S(1)}, f32[128,2048]{0,1:T(8,128)S(1)}, u32[]{:S(2)}, u32[]{:S(2)}) collective-permute-start(f32[128,2048]{0,1:T(8,128)S(1)} %collective-permute-done.19), channel_id=1, source_target_pairs={{0,15},{1,0},{2,1},{3,2},{4,3},{5,4},{6,5},{7,6},{8,7},{9,8},{10,9... | collective-permute-start | bytes 3145736 | tf_op jit(solution)/shard_map/ppermute | solution.py:29
  774.6 5.2 copy-start.20
  774.6 24.1 %collective-permute-start.22 = (f32[128,2048]{0,1:T(8,128)S(1)}, f32[128,2048]{0,1:T(8,128)}, u32[]{:S(2)}, u32[]{:S(2)}) collective-permute-start(f32[128,2048]{0,1:T(8,128)S(1)} %collective-permute-done.20), channel_id=1, source_target_pairs={{0,1},{1,2},{2,3},{3,4},{4,5},{5,6},{6,7},{7,8},{8,9},{9,10},{10,1... | collective-permute-start | bytes 3145736 | tf_op jit(solution)/shard_map/ppermute | solution.py:24
  774.6 34.9 %copy-start.18 = (f32[128,2048]{0,1:T(8,128)}, f32[128,2048]{0,1:T(8,128)S(1)}, u32[]{:S(2)}) copy-start(f32[128,2048]{0,1:T(8,128)S(1)} %collective-permute-done.21) | copy-start | bytes 3145732
  774.6 28.0 %collective-permute-start.23 = (f32[128,2048]{0,1:T(8,128)S(1)}, f32[128,2048]{0,1:T(8,128)}, u32[]{:S(2)}, u32[]{:S(2)}) collective-permute-start(f32[128,2048]{0,1:T(8,128)S(1)} %collective-permute-done.21), channel_id=1, source_target_pairs={{0,15},{1,0},{2,1},{3,2},{4,3},{5,4},{6,5},{7,6},{8,7},{9,8},{10,9... | collective-permute-start | bytes 3145736 | tf_op jit(solution)/shard_map/ppermute | solution.py:29
  798.7 23.5 %collective-permute-start.24 = (f32[128,2048]{0,1:T(8,128)}, f32[128,2048]{0,1:T(8,128)}, u32[]{:S(2)}, u32[]{:S(2)}) collective-permute-start(f32[128,2048]{0,1:T(8,128)} %collective-permute-done.22), channel_id=1, source_target_pairs={{0,1},{1,2},{2,3},{3,4},{4,5},{5,6},{6,7},{7,8},{8,9},{9,10},{10,1... | collective-permute-start | bytes 3145736 | tf_op jit(solution)/shard_map/ppermute | solution.py:24
  799.8 9.7 collective-permute-start.31
  802.6 37.6 %collective-permute-start.25 = (f32[128,2048]{0,1:T(8,128)}, f32[128,2048]{0,1:T(8,128)}, u32[]{:S(2)}, u32[]{:S(2)}) collective-permute-start(f32[128,2048]{0,1:T(8,128)} %collective-permute-done.23), channel_id=1, source_target_pairs={{0,15},{1,0},{2,1},{3,2},{4,3},{5,4},{6,5},{7,6},{8,7},{9,8},{10,9... | collective-permute-start | bytes 3145736 | tf_op jit(solution)/shard_map/ppermute | solution.py:29
  822.2 28.4 %collective-permute-start.26 = (f32[128,2048]{0,1:T(8,128)}, f32[128,2048]{0,1:T(8,128)}, u32[]{:S(2)}, u32[]{:S(2)}) collective-permute-start(f32[128,2048]{0,1:T(8,128)} %collective-permute-done.24), channel_id=1, source_target_pairs={{0,1},{1,2},{2,3},{3,4},{4,5},{5,6},{6,7},{7,8},{8,9},{9,10},{10,1... | collective-permute-start | bytes 3145736 | tf_op jit(solution)/shard_map/ppermute | solution.py:24
  840.2 23.3 %collective-permute-start.27 = (f32[128,2048]{0,1:T(8,128)}, f32[128,2048]{0,1:T(8,128)}, u32[]{:S(2)}, u32[]{:S(2)}) collective-permute-start(f32[128,2048]{0,1:T(8,128)} %collective-permute-done.25), channel_id=1, source_target_pairs={{0,15},{1,0},{2,1},{3,2},{4,3},{5,4},{6,5},{7,6},{8,7},{9,8},{10,9... | collective-permute-start | bytes 3145736 | tf_op jit(solution)/shard_map/ppermute | solution.py:29
  850.6 25.2 %collective-permute-start.28 = (f32[128,2048]{0,1:T(8,128)}, f32[128,2048]{0,1:T(8,128)}, u32[]{:S(2)}, u32[]{:S(2)}) collective-permute-start(f32[128,2048]{0,1:T(8,128)} %collective-permute-done.26), channel_id=1, source_target_pairs={{0,1},{1,2},{2,3},{3,4},{4,5},{5,6},{6,7},{7,8},{8,9},{9,10},{10,1... | collective-permute-start | bytes 3145736 | tf_op jit(solution)/shard_map/ppermute | solution.py:24
  863.5 22.5 %collective-permute-start.29 = (f32[128,2048]{0,1:T(8,128)}, f32[128,2048]{0,1:T(8,128)}, u32[]{:S(2)}, u32[]{:S(2)}) collective-permute-start(f32[128,2048]{0,1:T(8,128)} %collective-permute-done.27), channel_id=1, source_target_pairs={{0,15},{1,0},{2,1},{3,2},{4,3},{5,4},{6,5},{7,6},{8,7},{9,8},{10,9... | collective-permute-start | bytes 3145736 | tf_op jit(solution)/shard_map/ppermute | solution.py:29
  875.8 21.4 %collective-permute-start.30 = (f32[128,2048]{0,1:T(8,128)}, f32[128,2048]{0,1:T(8,128)}, u32[]{:S(2)}, u32[]{:S(2)}) collective-permute-start(f32[128,2048]{0,1:T(8,128)} %collective-permute-done.28), channel_id=1, source_target_pairs={{0,1},{1,2},{2,3},{3,4},{4,5},{5,6},{6,7},{7,8},{8,9},{9,10},{10,1... | collective-permute-start | bytes 3145736 | tf_op jit(solution)/shard_map/ppermute | solution.py:24
  892.0 126.1 %copy-start.25 = (f32[128,128]{1,0:T(8,128)S(1)}, f32[128,128]{1,0:T(8,128)}, u32[]{:S(2)}) copy-start(f32[128,128]{1,0:T(8,128)} %get-tuple-element.136) | copy-start | bytes 196612
  899.9 199.3 %copy-start.24 = (f32[128,128]{1,0:T(8,128)S(1)}, f32[128,128]{1,0:T(8,128)}, u32[]{:S(2)}) copy-start(f32[128,128]{1,0:T(8,128)} %get-tuple-element.134) | copy-start | bytes 196612
  899.9 199.5 %copy-start.26 = (f32[128,128]{1,0:T(8,128)S(1)}, f32[128,128]{1,0:T(8,128)}, u32[]{:S(2)}) copy-start(f32[128,128]{1,0:T(8,128)} %get-tuple-element.132) | copy-start | bytes 196612
  912.4 190.2 %copy-start.27 = (f32[128,128]{1,0:T(8,128)S(1)}, f32[128,128]{1,0:T(8,128)}, u32[]{:S(2)}) copy-start(f32[128,128]{1,0:T(8,128)} %get-tuple-element.130) | copy-start | bytes 196612
  912.4 191.8 %copy-start.28 = (f32[128,128]{1,0:T(8,128)S(1)}, f32[128,128]{1,0:T(8,128)}, u32[]{:S(2)}) copy-start(f32[128,128]{1,0:T(8,128)} %get-tuple-element.128) | copy-start | bytes 196612
  912.4 193.4 %copy-start.29 = (f32[128,128]{1,0:T(8,128)S(1)}, f32[128,128]{1,0:T(8,128)}, u32[]{:S(2)}) copy-start(f32[128,128]{1,0:T(8,128)} %get-tuple-element.126) | copy-start | bytes 196612
  912.4 16.5 %collective-permute-start.32 = (f32[128,2048]{0,1:T(8,128)S(1)}, f32[128,2048]{0,1:T(8,128)S(1)}, u32[]{:S(2)}, u32[]{:S(2)}) collective-permute-start(f32[128,2048]{0,1:T(8,128)S(1)} %bitcast_add_fusion), channel_id=1, source_target_pairs={{0,32},{16,48},{32,0},{48,16},{64,96},{80,112},{96,64},{112,80},{1... | collective-permute-start | bytes 3145736 | tf_op jit(solution)/shard_map/ppermute | solution.py:42
  929.7 135.8 %all-gather.24.cloned.1.call-start = ((), (), s32[]{:S(2)}) async-start(), calls=%async_computation.7 | async-start | bytes 1114112 | tf_op jit(solution)/shard_map/all_gather | solution.py:50
  1017.8 127.6 %all-gather.26.cloned.1.call-start = ((), (), s32[]{:S(2)}) async-start(), calls=%async_computation.8 | async-start | bytes 1114112 | tf_op jit(solution)/shard_map/all_gather | solution.py:50
  (11 other events, 12.5 us)
Sparse Core Ops, SparseCore 0:
  11.0 50.7 all-gather.9
  92.0 47.5 all-gather.11
  170.7 47.5 all-gather.13
  462.9 49.2 all-gather.15
  543.4 47.5 all-gather.17
  623.3 47.5 all-gather.19
  929.8 49.4 all-gather.21
  1017.9 47.5 all-gather.23
  1097.8 47.5 all-gather.25
